TPU v7x, 256 devices: a whole 4x4x8 slice. The times are simulated.
256 devices in a mesh: wave: 64 (over z, y, core), lev: 4 (over x).
Axes of the slice: x: 4, y: 4, z: 8, core: 2. Of those that a mesh axis runs over, the one named last changes fastest.
Arguments:
- coefficients: bfloat16 [640, 2, 128, 640], P('wave', None, 'lev'), may hold values from -0.1796875 to 0.1796875
- legendre: bfloat16 [640, 2, 640, 512], P('wave'), may hold values from -0.25 to 0.25
- pair_wave: int32 [640], replicated, may hold values from 0 to 639, each once
- row_points: int32 [512], replicated, may hold values from 20 to 5136, as said below
- layer_logpressure_factor: float32 [16], replicated, may hold values from 0.05 to 0.5
Outputs:
- physical_space_values: bfloat16 [1024, 64, 5248], P('wave', 'lev')
- geopotential: bfloat16 [1024, 16, 5248], P('wave', 'lev')
Inputs may be any that keep to these rules, and one draw needn't show every extreme that they name: Pair q holds zonal wavenumbers pair_wave[q] and 1279 - pair_wave[q]; each value appears once. `row_points`: the northern rows from the pole toward the equator: 16 + 4 j points for distinct octahedral rows j of 1 to 1280, strictly rising; the last row is j = 1280.
All inputs are finite; a program needn't handle non-finite values.
Results may differ from a plain program's by a relative error of at most 0.0062.
Values may be sent and summed in bfloat16 or wider, within the bound.
No kernel may reach another device: no remote copies, remote signals or barrier semaphores. Data moves between devices by JAX's collectives and lax.ppermute only.
A program may use at most 128 MiB of HBM per device.

v0:
```python
import jax
import jax.numpy as jnp
from jax import lax
from jax.sharding import PartitionSpec as P

TRUNC = 1279
QUANTITY_COUNT = 4
LCAP = 5248


two_pi = 6.283185307179586
group_blocks = 8


def prefix(shard, axis, combine, identity):
    size, mine = (lax.axis_size(axis), lax.axis_index(axis))
    everything = lax.all_gather(shard, axis)
    start = jnp.broadcast_to(jnp.asarray(identity, shard.dtype), shard.shape)

    def lap(k, before):
        at = size - 1 - k
        reached = at > mine
        new = combine(before, everything[at])
        return jnp.where(reached, new, before)

    return lax.fori_loop(0, size, lap, start)


def pair_masks(low_waves, pack_width):
    parity = jnp.arange(2, dtype=jnp.int32)
    low_count = (TRUNC - low_waves[:, None] - parity[None, :]) // 2 + 1
    high_count = (low_waves[:, None] - parity[None, :]) // 2 + 1
    pack_index = jnp.arange(pack_width, dtype=jnp.int32)[None, None, :]
    low_mask = pack_index < low_count[:, :, None]
    high_mask = (pack_index >= low_count[:, :, None]) & (
        pack_index < (low_count + high_count)[:, :, None]
    )
    return jnp.stack([low_mask, high_mask], axis=2)


def angle_of(residue, points):
    return residue.astype(jnp.float32) * (jnp.float32(two_pi) / points.astype(jnp.float32))


def synth_row(fourier_row, points, wave_numbers):
    fields = fourier_row.shape[0]
    slots = wave_numbers.shape[0]
    span = 128 * group_blocks
    padded_width = (LCAP + span - 1) // span * span
    wave_limit = jnp.minimum(TRUNC, (points - 1) // 2)
    kept_coef = fourier_row * (wave_numbers <= wave_limit).astype(jnp.float32)[None, None, :]
    real_part = kept_coef[:, 0, :]
    imag_part = kept_coef[:, 1, :]
    offsets = jnp.arange(128, dtype=jnp.int32)
    base_angle = angle_of(wave_numbers[:, None] * offsets[None, :] % points, points)
    base_table = jnp.concatenate([jnp.cos(base_angle), -jnp.sin(base_angle)], axis=0).astype(
        jnp.bfloat16
    )
    groups = (points + span - 1) // span
    block_offsets = jnp.arange(group_blocks, dtype=jnp.int32)

    def group_step(group_index, row_out):
        block_index = group_blocks * group_index + block_offsets
        block_shift = 128 * block_index % points
        twist = angle_of(block_shift[:, None] * wave_numbers[None, :] % points, points)
        twist_cos = jnp.cos(twist)[:, None, :]
        twist_sin = jnp.sin(twist)[:, None, :]
        twisted = jnp.concatenate(
            [
                real_part[None] * twist_cos - imag_part[None] * twist_sin,
                real_part[None] * twist_sin + imag_part[None] * twist_cos,
            ],
            axis=2,
        ).astype(jnp.bfloat16)
        twisted = twisted.reshape(group_blocks * fields, 2 * slots)
        block_values = jnp.dot(twisted, base_table, preferred_element_type=jnp.float32)
        block_values = jnp.transpose(
            block_values.reshape(group_blocks, fields, 128), (1, 0, 2)
        ).reshape(fields, span)
        position = span * group_index + jnp.arange(span, dtype=jnp.int32)
        block_values = jnp.where(position[None, :] < points, block_values, 0.0)
        return lax.dynamic_update_slice_in_dim(
            row_out, block_values.astype(jnp.bfloat16), span * group_index, 1
        )

    row_full = lax.fori_loop(0, groups, group_step, jnp.zeros((fields, padded_width), jnp.bfloat16))
    return row_full[:, :LCAP]


def synth_band(fourier_band, lengths, wave_numbers):

    def one_row(row_pack):
        return synth_row(row_pack[0], row_pack[1], wave_numbers)

    return lax.map(one_row, (fourier_band, lengths))


def add_terms(earlier, later):
    return earlier + later


def local(coefficients, legendre, pair_wave, row_points, layer_logpressure_factor):
    wave_count = lax.axis_size("wave")
    wave_rank = lax.axis_index("wave")
    pair_local = coefficients.shape[0]
    pack_width = coefficients.shape[3]
    fields = coefficients.shape[2] // 2
    half_rows = legendre.shape[3]
    all_rows = 2 * half_rows
    band_rows = all_rows // wave_count
    my_pairs = lax.dynamic_slice_in_dim(pair_wave, wave_rank * pair_local, pair_local)
    selection = pair_masks(my_pairs, pack_width).astype(jnp.bfloat16)
    selected = coefficients[:, :, None, :, :] * selection[:, :, :, None, :]
    selected = selected.reshape(pair_local, 2, 2, fields, 2, pack_width)
    legendre_sums = jnp.einsum(
        "qehfsk,qekt->etfsqh", selected, legendre, preferred_element_type=jnp.float32
    )
    north_rows = legendre_sums[0] + legendre_sums[1]
    south_rows = jnp.flip(legendre_sums[0] - legendre_sums[1], 0)
    fourier = jnp.concatenate([north_rows, south_rows], 0).reshape(
        all_rows, fields, 2, 2 * pair_local
    )
    wave_numbers = jnp.stack([pair_wave, TRUNC - pair_wave], axis=1).reshape(-1)
    points_all = jnp.concatenate([row_points, jnp.flip(row_points)])
    rows_here = wave_rank * band_rows + jnp.arange(band_rows, dtype=jnp.int32)
    lengths = points_all[rows_here]
    inverse_transformed_values = synth_band(
        lax.all_to_all(fourier, "wave", split_axis=0, concat_axis=3, tiled=True),
        lengths,
        wave_numbers,
    )
    heat_state_values = inverse_transformed_values[:, 0::QUANTITY_COUNT, :].astype(jnp.float32)
    device_layer_index = heat_state_values.shape[1]
    layer_depth_factor = lax.dynamic_slice_in_dim(
        layer_logpressure_factor, lax.axis_index("lev") * device_layer_index, device_layer_index
    )
    scaled_heat_values = heat_state_values * layer_depth_factor[None, :, None]
    underlying_partial_totals = jnp.flip(jnp.cumsum(jnp.flip(scaled_heat_values, 1), axis=1), 1)
    deeper = prefix(
        underlying_partial_totals[:, 0, :],
        "lev",
        add_terms,
        jnp.zeros_like(underlying_partial_totals[:, 0, :]),
    )
    geopotential = (underlying_partial_totals + deeper[:, None, :]).astype(jnp.bfloat16)
    return (inverse_transformed_values, geopotential)


def solution(mesh):
    return jax.shard_map(
        local,
        mesh=mesh,
        in_specs=(P("wave", None, "lev", None), P("wave", None, None, None), P(), P(), P()),
        out_specs=(P("wave", "lev", None), P("wave", "lev", None)),
        check_vma=False,
    )
```

profile of v0, /device:TPU:2, one launch (start us, length us, event | category | flops | bytes accessed | tf_op | source)
XLA Modules:
  0.0 655.5 jit_solution(16467618272180760468)
XLA Ops:
  7.2 2.2 mul.229
  10.0 6.0 fusion.27
  17.4 2.1 rev.16
  21.5 14.0 %copy.39 = f32[1024,16,2,20]{3,1,2,0:T(8,128)} copy(f32[1024,16,2,20]{0,1,2,3:T(8,128)S(1)} %bitcast.78) | data formatting | bytes 5242880 | tf_op jit(solution)/shard_map/reshape | solution.py:120
  35.5 19.8 %reshape.280 = f32[64,1,10240]{2,1,0:T(1,128)} reshape(f32[1024,2,16,20]{3,2,1,0:T(8,128)} %bitcast.76) | data formatting | bytes 5242880
  55.2 12.2 %all-to-all-start = ((f32[64,1,10240]{2,1,0:T(1,128)}), f32[64,1,10240]{2,1,0:T(1,128)S(1)}, u32[]{:S(2)}, u32[]{:S(2)}) async-start(f32[64,1,10240]{2,1,0:T(1,128)} %reshape.280), calls=%async_computation | async-start | bytes 5242880 | tf_op jit(solution)/shard_map/all_to_all | solution.py:128
  71.9 58.2 %all-to-all-done = f32[64,1,10240]{2,1,0:T(1,128)S(1)} async-done(((f32[64,1,10240]{2,1,0:T(1,128)}), f32[64,1,10240]{2,1,0:T(1,128)S(1)}, u32[]{:S(2)}, u32[]{:S(2)}) %all-to-all-start) | async-done | bytes 2621472 | tf_op jit(solution)/shard_map/all_to_all | solution.py:128
  130.6 9.0 %reduce = f32[64,10240]{1,0:T(8,128)} reduce(f32[64,1,10240]{2,1,0:T(1,128)S(1)} %all-to-all-done, f32[]{:T(128)} %broadcast.404), dimensions={1}, to_apply=%all_to_all.13.reduce_sub_computation | reduce | bytes 5242884 | tf_op jit(solution)/shard_map/all_to_all | solution.py:128
  139.6 21.8 %reshape.281 = f32[1024,2,16,20]{3,2,1,0:T(8,128)} reshape(f32[64,10240]{1,0:T(8,128)} %reduce) | data formatting | bytes 5242880
  161.4 17.7 %copy.41 = f32[16,16,2,64,20]{4,3,1,2,0:T(8,128)} copy(f32[16,16,2,64,20]{4,1,2,0,3:T(8,128)} %bitcast.77) | data formatting | bytes 5242880 | tf_op jit(solution)/shard_map/all_to_all | solution.py:128
  179.1 15.7 %all_to_all.16 = f32[16,16,2,1280]{3,1,2,0:T(8,128)} reshape(f32[16,16,2,64,20]{4,3,1,2,0:T(8,128)} %copy.41) | data formatting | bytes 5242880 | tf_op jit(solution)/shard_map/all_to_all | solution.py:128
  194.8 287.7 %while.63 = (s32[]{:T(128)}, bf16[16,16,5248]{2,1,0:T(8,128)(2,1)}, s32[16]{0:T(128)S(1)}, f32[16,16,2,1280]{3,1,2,0:T(8,128)}, s32[1280]{0:T(1024)S(1)}, /*inde...) while((s32[]{:T(128)}, bf16[16,16,5248]{2,1,0:T(8,128)(2,1)}, ...), condition=%wide.wide.region_3.4_spmd, body=%wide.wide.region_0.3_spmd.sunk | while | flops 90112632 | bytes 5585436 | solution.py:95
  197.3 9.3 %cosine_convert_fusion.3 = (bf16[1280,128]{1,0:T(8,128)(2,1)S(1)}, bf16[1280,128]{1,0:T(8,128)(2,1)S(1)}) fusion(f32[]{:T(128)} %div.105, s32[]{:T(128)} %select_n.224, s32[1280]{0:T(1024)S(1)} %get-tuple-element.886, pred[]{:T(512)} %lt.230), kind=kLoop, calls=%fused_computation.33.clone.clone.1 | loop fusion | flops 2129920 | bytes 660489 | tf_op jit(solution)/shard_map/convert.2
  210.1 2.0 while.64
  215.2 9.3 %cosine_convert_fusion.3 = (bf16[1280,128]{1,0:T(8,128)(2,1)S(1)}, bf16[1280,128]{1,0:T(8,128)(2,1)S(1)}) fusion(f32[]{:T(128)} %div.105, s32[]{:T(128)} %select_n.224, s32[1280]{0:T(1024)S(1)} %get-tuple-element.886, pred[]{:T(512)} %lt.230), kind=kLoop, calls=%fused_computation.33.clone.clone.1 | loop fusion | flops 2129920 | bytes 660489 | tf_op jit(solution)/shard_map/convert.2
  228.1 2.0 while.64
  233.2 9.3 %cosine_convert_fusion.3 = (bf16[1280,128]{1,0:T(8,128)(2,1)S(1)}, bf16[1280,128]{1,0:T(8,128)(2,1)S(1)}) fusion(f32[]{:T(128)} %div.105, s32[]{:T(128)} %select_n.224, s32[1280]{0:T(1024)S(1)} %get-tuple-element.886, pred[]{:T(512)} %lt.230), kind=kLoop, calls=%fused_computation.33.clone.clone.1 | loop fusion | flops 2129920 | bytes 660489 | tf_op jit(solution)/shard_map/convert.2
  246.0 2.0 while.64
  251.2 9.3 %cosine_convert_fusion.3 = (bf16[1280,128]{1,0:T(8,128)(2,1)S(1)}, bf16[1280,128]{1,0:T(8,128)(2,1)S(1)}) fusion(f32[]{:T(128)} %div.105, s32[]{:T(128)} %select_n.224, s32[1280]{0:T(1024)S(1)} %get-tuple-element.886, pred[]{:T(512)} %lt.230), kind=kLoop, calls=%fused_computation.33.clone.clone.1 | loop fusion | flops 2129920 | bytes 660489 | tf_op jit(solution)/shard_map/convert.2
  264.0 2.0 while.64
  269.2 9.3 %cosine_convert_fusion.3 = (bf16[1280,128]{1,0:T(8,128)(2,1)S(1)}, bf16[1280,128]{1,0:T(8,128)(2,1)S(1)}) fusion(f32[]{:T(128)} %div.105, s32[]{:T(128)} %select_n.224, s32[1280]{0:T(1024)S(1)} %get-tuple-element.886, pred[]{:T(512)} %lt.230), kind=kLoop, calls=%fused_computation.33.clone.clone.1 | loop fusion | flops 2129920 | bytes 660489 | tf_op jit(solution)/shard_map/convert.2
  282.0 2.0 while.64
  287.1 9.3 %cosine_convert_fusion.3 = (bf16[1280,128]{1,0:T(8,128)(2,1)S(1)}, bf16[1280,128]{1,0:T(8,128)(2,1)S(1)}) fusion(f32[]{:T(128)} %div.105, s32[]{:T(128)} %select_n.224, s32[1280]{0:T(1024)S(1)} %get-tuple-element.886, pred[]{:T(512)} %lt.230), kind=kLoop, calls=%fused_computation.33.clone.clone.1 | loop fusion | flops 2129920 | bytes 660489 | tf_op jit(solution)/shard_map/convert.2
  300.0 2.0 while.64
  305.1 9.3 %cosine_convert_fusion.3 = (bf16[1280,128]{1,0:T(8,128)(2,1)S(1)}, bf16[1280,128]{1,0:T(8,128)(2,1)S(1)}) fusion(f32[]{:T(128)} %div.105, s32[]{:T(128)} %select_n.224, s32[1280]{0:T(1024)S(1)} %get-tuple-element.886, pred[]{:T(512)} %lt.230), kind=kLoop, calls=%fused_computation.33.clone.clone.1 | loop fusion | flops 2129920 | bytes 660489 | tf_op jit(solution)/shard_map/convert.2
  318.0 2.0 while.64
  323.1 9.3 %cosine_convert_fusion.3 = (bf16[1280,128]{1,0:T(8,128)(2,1)S(1)}, bf16[1280,128]{1,0:T(8,128)(2,1)S(1)}) fusion(f32[]{:T(128)} %div.105, s32[]{:T(128)} %select_n.224, s32[1280]{0:T(1024)S(1)} %get-tuple-element.886, pred[]{:T(512)} %lt.230), kind=kLoop, calls=%fused_computation.33.clone.clone.1 | loop fusion | flops 2129920 | bytes 660489 | tf_op jit(solution)/shard_map/convert.2
  335.9 2.0 while.64
  341.1 9.3 %cosine_convert_fusion.3 = (bf16[1280,128]{1,0:T(8,128)(2,1)S(1)}, bf16[1280,128]{1,0:T(8,128)(2,1)S(1)}) fusion(f32[]{:T(128)} %div.105, s32[]{:T(128)} %select_n.224, s32[1280]{0:T(1024)S(1)} %get-tuple-element.886, pred[]{:T(512)} %lt.230), kind=kLoop, calls=%fused_computation.33.clone.clone.1 | loop fusion | flops 2129920 | bytes 660489 | tf_op jit(solution)/shard_map/convert.2
  353.9 2.0 while.64
  359.1 9.3 %cosine_convert_fusion.3 = (bf16[1280,128]{1,0:T(8,128)(2,1)S(1)}, bf16[1280,128]{1,0:T(8,128)(2,1)S(1)}) fusion(f32[]{:T(128)} %div.105, s32[]{:T(128)} %select_n.224, s32[1280]{0:T(1024)S(1)} %get-tuple-element.886, pred[]{:T(512)} %lt.230), kind=kLoop, calls=%fused_computation.33.clone.clone.1 | loop fusion | flops 2129920 | bytes 660489 | tf_op jit(solution)/shard_map/convert.2
  371.9 2.0 while.64
  377.0 9.3 %cosine_convert_fusion.3 = (bf16[1280,128]{1,0:T(8,128)(2,1)S(1)}, bf16[1280,128]{1,0:T(8,128)(2,1)S(1)}) fusion(f32[]{:T(128)} %div.105, s32[]{:T(128)} %select_n.224, s32[1280]{0:T(1024)S(1)} %get-tuple-element.886, pred[]{:T(512)} %lt.230), kind=kLoop, calls=%fused_computation.33.clone.clone.1 | loop fusion | flops 2129920 | bytes 660489 | tf_op jit(solution)/shard_map/convert.2
  389.9 2.0 while.64
  395.0 9.3 %cosine_convert_fusion.3 = (bf16[1280,128]{1,0:T(8,128)(2,1)S(1)}, bf16[1280,128]{1,0:T(8,128)(2,1)S(1)}) fusion(f32[]{:T(128)} %div.105, s32[]{:T(128)} %select_n.224, s32[1280]{0:T(1024)S(1)} %get-tuple-element.886, pred[]{:T(512)} %lt.230), kind=kLoop, calls=%fused_computation.33.clone.clone.1 | loop fusion | flops 2129920 | bytes 660489 | tf_op jit(solution)/shard_map/convert.2
  407.8 2.0 while.64
  413.0 9.3 %cosine_convert_fusion.3 = (bf16[1280,128]{1,0:T(8,128)(2,1)S(1)}, bf16[1280,128]{1,0:T(8,128)(2,1)S(1)}) fusion(f32[]{:T(128)} %div.105, s32[]{:T(128)} %select_n.224, s32[1280]{0:T(1024)S(1)} %get-tuple-element.886, pred[]{:T(512)} %lt.230), kind=kLoop, calls=%fused_computation.33.clone.clone.1 | loop fusion | flops 2129920 | bytes 660489 | tf_op jit(solution)/shard_map/convert.2
  425.8 2.0 while.64
  431.0 9.3 %cosine_convert_fusion.3 = (bf16[1280,128]{1,0:T(8,128)(2,1)S(1)}, bf16[1280,128]{1,0:T(8,128)(2,1)S(1)}) fusion(f32[]{:T(128)} %div.105, s32[]{:T(128)} %select_n.224, s32[1280]{0:T(1024)S(1)} %get-tuple-element.886, pred[]{:T(512)} %lt.230), kind=kLoop, calls=%fused_computation.33.clone.clone.1 | loop fusion | flops 2129920 | bytes 660489 | tf_op jit(solution)/shard_map/convert.2
  443.8 2.0 while.64
  449.0 9.3 %cosine_convert_fusion.3 = (bf16[1280,128]{1,0:T(8,128)(2,1)S(1)}, bf16[1280,128]{1,0:T(8,128)(2,1)S(1)}) fusion(f32[]{:T(128)} %div.105, s32[]{:T(128)} %select_n.224, s32[1280]{0:T(1024)S(1)} %get-tuple-element.886, pred[]{:T(512)} %lt.230), kind=kLoop, calls=%fused_computation.33.clone.clone.1 | loop fusion | flops 2129920 | bytes 660489 | tf_op jit(solution)/shard_map/convert.2
  461.8 2.0 while.64
  466.9 9.3 %cosine_convert_fusion.3 = (bf16[1280,128]{1,0:T(8,128)(2,1)S(1)}, bf16[1280,128]{1,0:T(8,128)(2,1)S(1)}) fusion(f32[]{:T(128)} %div.105, s32[]{:T(128)} %select_n.224, s32[1280]{0:T(1024)S(1)} %get-tuple-element.886, pred[]{:T(512)} %lt.230), kind=kLoop, calls=%fused_computation.33.clone.clone.1 | loop fusion | flops 2129920 | bytes 660489 | tf_op jit(solution)/shard_map/convert.2
  479.8 2.0 while.64
  482.4 2.2 copy.44
  484.9 4.0 fusion.36
  489.7 153.3 %all-gather.3.cloned.1.call-done = f32[64,1,5248]{2,0,1:T(8,128)} async-done(((f32[16,1,5248]{2,0,1:T(8,128)}), f32[64,1,5248]{2,0,1:T(8,128)}) %all-gather.3.cloned.1.call-update) | async-done | bytes 1343504 | tf_op jit(solution)/shard_map/all_gather | solution.py:17
  643.0 4.4 while.61
  (263 shorter events, 101.4 us)
Async XLA Ops:
  7.2 2.3 copy-start
  55.2 15.8 %copy-start.1 = (s32[512]{0:T(512)S(1)}, s32[512]{0:T(512)}, u32[]{:S(2)}) copy-start(s32[512]{0:T(512)} %param.14) | copy-start | bytes 6148
  55.2 16.6 %copy-start.2 = (f32[16]{0:T(128)S(1)}, f32[16]{0:T(128)}, u32[]{:S(2)}) copy-start(f32[16]{0:T(128)} %param.15) | copy-start | bytes 196
  55.2 74.9 %all-to-all-start = ((f32[64,1,10240]{2,1,0:T(1,128)}), f32[64,1,10240]{2,1,0:T(1,128)S(1)}, u32[]{:S(2)}, u32[]{:S(2)}) async-start(f32[64,1,10240]{2,1,0:T(1,128)} %reshape.280), calls=%async_computation | async-start | bytes 5242880 | tf_op jit(solution)/shard_map/all_to_all | solution.py:128
  67.5 575.5 %all-gather.3.cloned.1.call-start = ((), (), s32[]{:S(2)}) async-start(), calls=%async_computation.1 | async-start | bytes 1679360 | tf_op jit(solution)/shard_map/all_gather | solution.py:17
Sparse Core Ops, SparseCore 0:
  489.8 153.1 all-gather.2
where the time goes:
time: 659 us; the launch traced here: 655 us
  other arithmetic  212 us (32%)
  waiting for transfers between devices  212 us (32%)
  local copies, waits for them, and re-layouts  142 us (22%)
  loops' own time  52.6 us (8%)
  between operations  14.2 us (2%)
  starting transfers between devices  12.5 us (2%)
  matrix products  11.2 us (2%)
    all_gather x1, waiting for transfers between devices, prefix(): everything = lax.all_gather(shard, axis)  153 us
    another operation x32, other arithmetic  152 us
    all_to_all x1, waiting for transfers between devices, local(): lax.all_to_all(fourier, 'wave', split_axis=0, concat_axis=3, tiled=True)  58.2 us
    another operation x1, loops' own time, synth_band(): return lax.map(one_row, (fourier_band, lengths))  51.6 us
    unnamed x9, local copies, waits for them, and re-layouts  42.7 us
    all_to_all x3, local copies, waits for them, and re-layouts, local(): lax.all_to_all(fourier, 'wave', split_axis=0, concat_axis=3, tiled=True)  33.9 us
    mul x16, local copies, waits for them, and re-layouts, group_step(): block_shift[:, None] * wave_numbers[None, :] % points  18.9 us
    mul x16, other arithmetic, synth_row(): fourier_row * (wave_numbers <= wave_limit).astype(jnp.float32)[None, None...  15 us
  transfers between devices with their start and end apart: 2, of which 2 were waited for; matrix products, arithmetic and copies ran while one was open for 1% of the time, Pallas kernels for 0%

commit v1 on v0

v1 whole, which is shorter than its diff:
```python
import jax
import jax.numpy as jnp
from jax import lax
from jax.sharding import PartitionSpec as P

TRUNC = 1279
QUANTITY_COUNT = 4
LCAP = 5248
BLOCK = 128
BLOCKS = LCAP // BLOCK

two_pi = 6.283185307179586


def pair_masks(low_waves, pack_width):
    parity = jnp.arange(2, dtype=jnp.int32)
    low_count = (TRUNC - low_waves[:, None] - parity[None, :]) // 2 + 1
    high_count = (low_waves[:, None] - parity[None, :]) // 2 + 1
    pack_index = jnp.arange(pack_width, dtype=jnp.int32)[None, None, :]
    low_mask = pack_index < low_count[:, :, None]
    high_mask = (pack_index >= low_count[:, :, None]) & (
        pack_index < (low_count + high_count)[:, :, None]
    )
    return jnp.stack([low_mask, high_mask], axis=2)


def residue(j, points):
    q = jnp.floor(j.astype(jnp.float32) / points.astype(jnp.float32)).astype(jnp.int32)
    r = j - q * points
    r = jnp.where(r < 0, r + points, r)
    return jnp.where(r >= points, r - points, r)


def phase(waves, steps, points):
    j = waves * steps
    rem = residue(j, points)
    angle = rem.astype(jnp.float32) * (jnp.float32(two_pi) / points.astype(jnp.float32))
    return jnp.cos(angle), jnp.sin(angle)


def times(a, b):
    return a[0] * b[0] - a[1] * b[1], a[1] * b[0] + a[0] * b[1]


def tables(wave_numbers, lengths):
    rows = lengths.shape[0]
    slots = wave_numbers.shape[0]
    w = wave_numbers[None, None, :]
    pts = lengths[:, None, None]
    low = phase(w, jnp.arange(16, dtype=jnp.int32)[None, :, None], pts)
    high = phase(w, 16 * jnp.arange(8, dtype=jnp.int32)[None, :, None], pts)
    cos_b, sin_b = times(
        (high[0][:, :, None, :], high[1][:, :, None, :]),
        (low[0][:, None, :, :], low[1][:, None, :, :]),
    )
    base_t = jnp.concatenate(
        [cos_b.reshape(rows, BLOCK, slots), -sin_b.reshape(rows, BLOCK, slots)], axis=2
    ).astype(jnp.bfloat16)
    near = phase(w, BLOCK * jnp.arange(8, dtype=jnp.int32)[None, :, None], pts)
    far = phase(w, 8 * BLOCK * jnp.arange(6, dtype=jnp.int32)[None, :, None], pts)
    cos_t, sin_t = times(
        (far[0][:, :, None, :], far[1][:, :, None, :]),
        (near[0][:, None, :, :], near[1][:, None, :, :]),
    )
    wave_limit = jnp.minimum(TRUNC, (lengths - 1) // 2)
    keep = (wave_numbers[None, :] <= wave_limit[:, None]).astype(jnp.float32)[:, None, :]
    cos_t = cos_t.reshape(rows, 48, slots)[:, :BLOCKS] * keep
    sin_t = sin_t.reshape(rows, 48, slots)[:, :BLOCKS] * keep
    return base_t, cos_t, sin_t


def synth_row(pack):
    fourier_row, base_t, cos_t, sin_t, points = pack
    fields = fourier_row.shape[0] // 2
    real_part = fourier_row[:fields]
    imag_part = fourier_row[fields:]
    c = cos_t[:, None, :]
    s = sin_t[:, None, :]
    twisted = jnp.concatenate(
        [real_part[None] * c - imag_part[None] * s, real_part[None] * s + imag_part[None] * c],
        axis=2,
    ).astype(jnp.bfloat16)
    values = jnp.einsum("bfs,ks->fbk", twisted, base_t, preferred_element_type=jnp.float32)
    values = values.reshape(fields, LCAP)
    position = jnp.arange(LCAP, dtype=jnp.int32)
    values = jnp.where(position[None, :] < points, values, 0.0)
    return values.astype(jnp.bfloat16)


def local(coefficients, legendre, pair_wave, row_points, layer_logpressure_factor):
    wave_count = lax.axis_size("wave")
    wave_rank = lax.axis_index("wave")
    pair_local, _, cols, pack_width = coefficients.shape
    fields = cols // 2
    half_rows = legendre.shape[3]
    all_rows = 2 * half_rows
    band_rows = all_rows // wave_count
    half_bands = half_rows // band_rows
    my_pairs = lax.dynamic_slice_in_dim(pair_wave, wave_rank * pair_local, pair_local)
    selection = pair_masks(my_pairs, pack_width).astype(jnp.bfloat16)
    coef = coefficients.reshape(pair_local, 2, fields, 2, pack_width).transpose(0, 1, 3, 2, 4)
    coef = coef.reshape(pair_local, 2, cols, pack_width)
    selected = coef[:, :, None, :, :] * selection[:, :, :, None, :]
    signs = jnp.array([[1.0, 1.0], [1.0, -1.0]], jnp.bfloat16)
    lhs = signs[None, :, :, None, None, None] * selected[:, None]
    sums = jnp.einsum("qaehci,qeit->atqhc", lhs, legendre, preferred_element_type=jnp.float32)
    sums = sums.reshape(2, half_bands, band_rows, pair_local * 2, cols)
    south = jnp.flip(sums[1], (0, 1))
    bands = jnp.concatenate([sums[0], south], 0)
    send = bands.transpose(0, 2, 1, 3).reshape(wave_count, pair_local * 2, band_rows * cols)
    got = lax.all_to_all(send, "wave", 0, 0, tiled=True)
    slots = got.shape[0] * got.shape[1]
    fourier = got.reshape(slots, band_rows * cols).T.reshape(band_rows, cols, slots)

    wave_numbers = jnp.stack([pair_wave, TRUNC - pair_wave], axis=1).reshape(-1)
    points_all = jnp.concatenate([row_points, jnp.flip(row_points)])
    lengths = lax.dynamic_slice_in_dim(points_all, wave_rank * band_rows, band_rows)
    base_t, cos_t, sin_t = tables(wave_numbers, lengths)
    values = lax.map(synth_row, (fourier, base_t, cos_t, sin_t, lengths), batch_size=4)

    heat_state_values = values[:, 0::QUANTITY_COUNT, :].astype(jnp.float32)
    device_layers = heat_state_values.shape[1]
    lev_rank = lax.axis_index("lev")
    layer_depth_factor = lax.dynamic_slice_in_dim(
        layer_logpressure_factor, lev_rank * device_layers, device_layers
    )
    scaled_heat_values = heat_state_values * layer_depth_factor[None, :, None]
    partial_totals = jnp.flip(jnp.cumsum(jnp.flip(scaled_heat_values, 1), axis=1), 1)
    everything = lax.all_gather(partial_totals[:, 0, :], "lev")
    lev_count = everything.shape[0]
    below = (jnp.arange(lev_count) > lev_rank).astype(jnp.float32)[:, None, None]
    deeper = jnp.sum(everything * below, axis=0)
    geopotential = (partial_totals + deeper[:, None, :]).astype(jnp.bfloat16)
    return (values, geopotential)


def solution(mesh):
    return jax.shard_map(
        local,
        mesh=mesh,
        in_specs=(P("wave", None, "lev", None), P("wave", None, None, None), P(), P(), P()),
        out_specs=(P("wave", "lev", None), P("wave", "lev", None)),
        check_vma=False,
    )
```

time: 659 us -> 278 us (0.42)
  waiting for transfers between devices: 212 us -> 64.9 us
  other arithmetic: 212 us -> 81.3 us
  local copies, waits for them, and re-layouts: 142 us -> 61.9 us
  loops' own time: 52.6 us -> 0.18 us
  matrix products: 11.2 us -> 40.9 us
    all_gather x1, waiting for transfers between devices: 153 us -> 22.9 us  [local(): everything = lax.all_gather(partial_totals[:, 0, :], 'lev')]
    another operation x32 -> x5, other arithmetic: 152 us -> 34.4 us
    another operation x18 -> x1, loops' own time: 52.6 us -> 0.18 us  [local(): lax.map(synth_row, (fourier, base_t, cos_t, sin_t, lengths), batch_size=4)]
    unnamed x9 -> x12, local copies, waits for them, and re-layouts: 42.7 us -> 3 us
    all_to_all x3 -> x0, local copies, waits for them, and re-layouts: 33.9 us -> none  [local(): lax.all_to_all(fourier, 'wave', split_axis=0, concat_axis=3, tiled=True)]
    dot_general x17 -> x5, matrix products: 11.2 us -> 40.9 us  [the longest x4 34.2 us: synth_row(): jnp.einsum('bfs,ks->fbk', twisted, base_t, preferred_element_type=jnp.flo...]
    all_to_all x1, waiting for transfers between devices: 58.2 us -> 42 us  [local(): got = lax.all_to_all(send, 'wave', 0, 0, tiled=True)]
    slice x17 -> x9, local copies, waits for them, and re-layouts: 0.96 us -> 17.2 us  [the longest x1 8.69 us: local(): heat_state_values = values[:, 0::QUANTITY_COUNT, :].astype(jnp.float32)]
  transfers between devices with their start and end apart: 2 -> 2, of which waited for: 2 -> 2; matrix products, arithmetic and copies ran while one was open for 1% -> 11% of each run, Pallas kernels for 0% -> 0%
where the time goes in v1:
time: 278 us; the launch traced here: 276 us
  other arithmetic  81.3 us (29%)
  waiting for transfers between devices  64.9 us (23%)
  local copies, waits for them, and re-layouts  61.9 us (22%)
  matrix products  40.9 us (15%)
  between operations  14.3 us (5%)
  starting transfers between devices  12.5 us (4%)
    all_to_all x1, waiting for transfers between devices, local(): got = lax.all_to_all(send, 'wave', 0, 0, tiled=True)  42 us
    another operation x5, other arithmetic  34.4 us
    dot_general x4, matrix products, synth_row(): jnp.einsum('bfs,ks->fbk', twisted, base_t, preferred_element_type=jnp.flo...  34.2 us
    all_gather x1, waiting for transfers between devices, local(): everything = lax.all_gather(partial_totals[:, 0, :], 'lev')  22.9 us
    cos x3, other arithmetic, phase(): return (jnp.cos(angle), jnp.sin(angle))  13.2 us
    all_to_all x1, starting transfers between devices, local(): got = lax.all_to_all(send, 'wave', 0, 0, tiled=True)  12.2 us
    transpose x1, local copies, waits for them, and re-layouts, local(): bands.transpose(0, 2, 1, 3)  9.48 us
    transpose x1, other arithmetic, local(): bands.transpose(0, 2, 1, 3)  9.15 us
  transfers between devices with their start and end apart: 2, of which 2 were waited for; matrix products, arithmetic and copies ran while one was open for 11% of the time, Pallas kernels for 0%

profile of v1, /device:TPU:2, one launch (start us, length us, event | category | flops | bytes accessed | tf_op | source)
XLA Modules:
  0.0 276.0 jit_solution(14441676474591296872)
XLA Ops:
  7.2 1.9 copy.29
  9.2 0.8 broadcast_subtract_fusion.1
  10.5 6.7 %fusion.18 = f32[2,512,10,2,32]{1,4,3,0,2:T(8,128)S(1)} fusion(bf16[10,2,640,512]{3,2,1,0:T(8,128)(2,1)} %param.9, bf16[10,2,2,32,640]{4,3,1,2,0:T(8,128)(2,1)S(1)} %broadcast_multiply_fusion, bf16[2,2]{1,0:T(2,128)(2,1)S(1)} %copy-done.1), kind=kOutput, calls=%fused_computation.38 | convolution fusion | flops 1679360000 | bytes 17367048 | tf_op jit(solution)/shard_map/qaehci,qeit->atqhc/dot_general | solution.py:106
  17.4 3.7 %copy.32 = f32[1,512,10,2,32]{4,1,3,2,0:T(8,128)} copy(f32[1,512,10,2,32]{1,4,3,0,2:T(8,128)S(1)} %get-tuple-element.82) | data formatting | bytes 2621440 | tf_op jit(solution)/shard_map/slice | solution.py:108
  21.1 8.4 %rev.16 = f32[32,16,20,32]{3,1,0,2:T(8,128)} reverse(f32[32,16,20,32]{3,1,0,2:T(8,128)} %bitcast.65), dimensions={0,1} | reverse | bytes 2621440 | tf_op jit(solution)/shard_map/jit(_flip)/rev | solution.py:108
  29.5 3.6 %copy.31 = f32[1,512,10,2,32]{4,1,3,2,0:T(8,128)} copy(f32[1,512,10,2,32]{1,4,3,0,2:T(8,128)S(1)} %get-tuple-element.81) | data formatting | bytes 2621440 | tf_op jit(solution)/shard_map/slice | solution.py:109
  33.1 9.2 %maximum_bitcast_fusion = f32[64,20,16,32]{3,2,0,1:T(8,128)} fusion(f32[32,16,20,32]{3,1,0,2:T(8,128)} %rev.16, f32[32,16,20,32]{3,1,0,2:T(8,128)} %bitcast.64), kind=kLoop, calls=%fused_computation.22 | loop fusion | flops 655360 | bytes 5242880 | tf_op jit(solution)/shard_map/transpose | solution.py:110
  42.3 9.5 %copy.33 = f32[64,20,16,32]{0,3,2,1:T(8,128)} copy(f32[64,20,16,32]{3,2,0,1:T(8,128)} %maximum_bitcast_fusion) | data formatting | bytes 5242880 | tf_op jit(solution)/shard_map/transpose | solution.py:110
  51.7 5.8 %copy.34 = f32[64,20,512]{2,1,0:T(8,128)} copy(f32[64,20,512]{0,2,1:T(8,128)} %bitcast.66) | data formatting | bytes 5242880 | tf_op jit(solution)/shard_map/reshape | solution.py:110
  57.5 12.2 %all-to-all-start = ((f32[64,20,512]{2,1,0:T(8,128)}), f32[64,20,512]{2,1,0:T(8,128)S(1)}, u32[]{:S(2)}, u32[]{:S(2)}) async-start(f32[64,20,512]{2,1,0:T(8,128)} %copy.34), calls=%async_computation | async-start | bytes 6291456 | tf_op jit(solution)/shard_map/all_to_all | solution.py:111
  70.9 0.7 broadcast_multiply_fusion.1
  71.7 2.6 fusion.48
  74.4 5.2 %fusion.46 = (f32[16,16,1280]{2,1,0:T(8,128)S(1)}, f32[16,16,1280]{2,1,0:T(8,128)S(1)}) fusion(f32[16]{0:T(128)S(1)} %broadcast_divide_fusion, s32[16]{0:T(128)S(1)} %get-tuple-element.68, f32[16]{0:T(128)S(1)} %convert_element_type.164, f32[16,1280]{1,0:T(8,128)S(1)} %get-tuple-element.104, s32[16,1280]{1,0:T(8,128)S(1)} %get-tuple-element.103), kind=kLoop, calls=%fused_computation.70 | loop fusion | flops 4259840 | bytes 2785472 | tf_op jit(solution)/shard_map/cos | solution.py:38
  79.6 5.4 %fusion.50 = (f32[16,8,1280]{2,1,0:T(8,128)S(1)}, f32[16,8,1280]{2,1,0:T(8,128)S(1)}, f32[16,8,1280]{2,1,0:T(8,128)S(1)}, f32[16,8,1280]{2,1,0:T(8,128)S(1)}) fusion(f32[16]{0:T(128)S(1)} %broadcast_divide_fusion, s32[16]{0:T(128)S(1)} %get-tuple-element.68, f32[16]{0:T(128)S(1)} %convert_element_type.164, f32[8,1280]{1,0:T(8,128)S(1)} %get-tuple-element.96, ...), kind=kLoop, calls=%fused_computation.74 | loop fusion | flops 4259840 | bytes 2785472 | tf_op jit(solution)/shard_map/cos | solution.py:38
  85.0 4.6 %subtract_convert_fusion.1 = (bf16[16,8,16,1280]{3,2,1,0:T(8,128)(2,1)S(1)}, bf16[16,8,16,1280]{3,2,1,0:T(8,128)(2,1)S(1)}) fusion(f32[16,16,1280]{2,1,0:T(8,128)S(1)} %get-tuple-element.84, f32[16,8,1280]{2,1,0:T(8,128)S(1)} %get-tuple-element.105, f32[16,16,1280]{2,1,0:T(8,128)S(1)} %get-tuple-element.83, f32[16,8,1280]{2,1,0:T(8,128)S(1)} %get-tuple-element.106), kind=kLoop, calls=%fused_computation.24 | loop fusion | flops 23592960 | bytes 14417920 | tf_op jit(solution)/shard_map/convert.5
  89.6 7.2 %pad_maximum_fusion = bf16[4,4,128,2560]{3,2,1,0:T(8,128)(2,1)} fusion(bf16[4,4,128,1280]{3,2,1,0:T(8,128)(2,1)S(1)} %bitcast.63, bf16[4,4,128,1280]{3,2,1,0:T(8,128)(2,1)S(1)} %bitcast.62), kind=kLoop, calls=%fused_computation.21 | loop fusion | flops 20971520 | bytes 20971520 | tf_op jit(solution)/shard_map/concatenate | solution.py:56
  96.8 1.1 add_bitcast_fusion
  97.9 3.7 %slice_multiply_fusion = (f32[16,41,1280]{2,1,0:T(8,128)}, f32[16,41,1280]{2,1,0:T(8,128)}) fusion(f32[16,48,1280]{2,1,0:T(8,128)S(1)} %get-tuple-element.79, f32[16,1280]{1,0:T(8,128)S(1)} %compare_convert_fusion, f32[16,48,1280]{2,1,0:T(8,128)S(1)} %get-tuple-element.80), kind=kLoop, calls=%fused_computation.25 | loop fusion | flops 1679360 | bytes 13516800 | tf_op jit(solution)/shard_map/mul | solution.py:68
  101.7 42.0 %all-to-all-done = f32[64,20,512]{2,1,0:T(8,128)S(1)} async-done(((f32[64,20,512]{2,1,0:T(8,128)}), f32[64,20,512]{2,1,0:T(8,128)S(1)}, u32[]{:S(2)}, u32[]{:S(2)}) %all-to-all-start) | async-done | bytes 2621472 | tf_op jit(solution)/shard_map/all_to_all | solution.py:111
  143.6 1.7 reshape.619
  145.4 3.2 %copy.35 = f32[512,1280]{1,0:T(8,128)} copy(f32[512,1280]{0,1:T(8,128)} %bitcast.69) | data formatting | bytes 5242880 | tf_op jit(solution)/shard_map/transpose | solution.py:113
  148.6 81.1 %while.10 = (s32[]{:T(128)}, bf16[4,4,16,5248]{3,2,1,0:T(8,128)(2,1)}, s32[4,4]{1,0:T(4,128)S(1)}, bf16[4,4,128,2560]{3,2,1,0:T(8,128)(2,1)}, f32[4,4,32,1280]{3...) while((s32[]{:T(128)}, bf16[4,4,16,5248]{3,2,1,0:T(8,128)(2,1)}, ...), condition=%wide.region_1.2_spmd, body=%wide.region_0.1_spmd.sunk | while | flops 1773761024 | bytes 43501712 | solution.py:119
  148.6 1.6 dynamic-slice_bitcast_fusion.5
  150.2 1.1 dynamic-slice_bitcast_fusion.6
  151.4 7.4 %subtract_convert_fusion.3 = (bf16[4,41,16,1280]{3,1,2,0:T(8,128)(2,1)}, bf16[4,41,16,1280]{3,1,2,0:T(8,128)(2,1)}) fusion(f32[4,41,1280]{2,1,0:T(8,128)S(1)} %get-tuple-element.160, f32[4,16,1280]{2,1,0:T(8,128)S(1)} %get-tuple-element.161, f32[4,41,1280]{2,1,0:T(8,128)S(1)} %get-tuple-element.162, f32[4,16,1280]{2,1,0:T(8,128)S(1)} %get-tuple-element.163), kind=kLoop, calls=%fused_computation.5.clone.1 | loop fusion | flops 26869760 | bytes 15769600 | tf_op jit(solution)/shard_map/convert
  158.8 8.6 %fusion.80 = bf16[4,16,41,128]{3,2,1,0:T(8,128)(2,1)S(1)} fusion(bf16[4,41,16,1280]{3,1,2,0:T(8,128)(2,1)} %get-tuple-element.164, bf16[4,41,16,1280]{3,1,2,0:T(8,128)(2,1)} %get-tuple-element.165, bf16[4,4,128,2560]{3,2,1,0:T(8,128)(2,1)} %get-tuple-element.185, s32[]{:T(128)} %get-tuple-element.174), kind=kOutput, calls=%fused_computation.8.clone.1 | convolution fusion | flops 1746534400 | bytes 19022336 | tf_op jit(solution)/shard_map/while/body/eval_jaxpr/vmap(bfs,ks->fbk)/dot_general | solution.py:83
  167.8 1.0 fusion.82
  168.9 1.6 dynamic-slice_bitcast_fusion.5
  170.5 1.1 dynamic-slice_bitcast_fusion.6
  171.7 7.4 %subtract_convert_fusion.3 = (bf16[4,41,16,1280]{3,1,2,0:T(8,128)(2,1)}, bf16[4,41,16,1280]{3,1,2,0:T(8,128)(2,1)}) fusion(f32[4,41,1280]{2,1,0:T(8,128)S(1)} %get-tuple-element.160, f32[4,16,1280]{2,1,0:T(8,128)S(1)} %get-tuple-element.161, f32[4,41,1280]{2,1,0:T(8,128)S(1)} %get-tuple-element.162, f32[4,16,1280]{2,1,0:T(8,128)S(1)} %get-tuple-element.163), kind=kLoop, calls=%fused_computation.5.clone.1 | loop fusion | flops 26869760 | bytes 15769600 | tf_op jit(solution)/shard_map/convert
  179.1 8.6 %fusion.80 = bf16[4,16,41,128]{3,2,1,0:T(8,128)(2,1)S(1)} fusion(bf16[4,41,16,1280]{3,1,2,0:T(8,128)(2,1)} %get-tuple-element.164, bf16[4,41,16,1280]{3,1,2,0:T(8,128)(2,1)} %get-tuple-element.165, bf16[4,4,128,2560]{3,2,1,0:T(8,128)(2,1)} %get-tuple-element.185, s32[]{:T(128)} %get-tuple-element.174), kind=kOutput, calls=%fused_computation.8.clone.1 | convolution fusion | flops 1746534400 | bytes 19022336 | tf_op jit(solution)/shard_map/while/body/eval_jaxpr/vmap(bfs,ks->fbk)/dot_general | solution.py:83
  188.1 1.0 fusion.82
  189.1 1.6 dynamic-slice_bitcast_fusion.5
  190.8 1.1 dynamic-slice_bitcast_fusion.6
  192.0 7.4 %subtract_convert_fusion.3 = (bf16[4,41,16,1280]{3,1,2,0:T(8,128)(2,1)}, bf16[4,41,16,1280]{3,1,2,0:T(8,128)(2,1)}) fusion(f32[4,41,1280]{2,1,0:T(8,128)S(1)} %get-tuple-element.160, f32[4,16,1280]{2,1,0:T(8,128)S(1)} %get-tuple-element.161, f32[4,41,1280]{2,1,0:T(8,128)S(1)} %get-tuple-element.162, f32[4,16,1280]{2,1,0:T(8,128)S(1)} %get-tuple-element.163), kind=kLoop, calls=%fused_computation.5.clone.1 | loop fusion | flops 26869760 | bytes 15769600 | tf_op jit(solution)/shard_map/convert
  199.4 8.6 %fusion.80 = bf16[4,16,41,128]{3,2,1,0:T(8,128)(2,1)S(1)} fusion(bf16[4,41,16,1280]{3,1,2,0:T(8,128)(2,1)} %get-tuple-element.164, bf16[4,41,16,1280]{3,1,2,0:T(8,128)(2,1)} %get-tuple-element.165, bf16[4,4,128,2560]{3,2,1,0:T(8,128)(2,1)} %get-tuple-element.185, s32[]{:T(128)} %get-tuple-element.174), kind=kOutput, calls=%fused_computation.8.clone.1 | convolution fusion | flops 1746534400 | bytes 19022336 | tf_op jit(solution)/shard_map/while/body/eval_jaxpr/vmap(bfs,ks->fbk)/dot_general | solution.py:83
  208.4 1.0 fusion.82
  209.4 1.6 dynamic-slice_bitcast_fusion.5
  211.0 1.1 dynamic-slice_bitcast_fusion.6
  212.2 7.4 %subtract_convert_fusion.3 = (bf16[4,41,16,1280]{3,1,2,0:T(8,128)(2,1)}, bf16[4,41,16,1280]{3,1,2,0:T(8,128)(2,1)}) fusion(f32[4,41,1280]{2,1,0:T(8,128)S(1)} %get-tuple-element.160, f32[4,16,1280]{2,1,0:T(8,128)S(1)} %get-tuple-element.161, f32[4,41,1280]{2,1,0:T(8,128)S(1)} %get-tuple-element.162, f32[4,16,1280]{2,1,0:T(8,128)S(1)} %get-tuple-element.163), kind=kLoop, calls=%fused_computation.5.clone.1 | loop fusion | flops 26869760 | bytes 15769600 | tf_op jit(solution)/shard_map/convert
  219.7 8.6 %fusion.80 = bf16[4,16,41,128]{3,2,1,0:T(8,128)(2,1)S(1)} fusion(bf16[4,41,16,1280]{3,1,2,0:T(8,128)(2,1)} %get-tuple-element.164, bf16[4,41,16,1280]{3,1,2,0:T(8,128)(2,1)} %get-tuple-element.165, bf16[4,4,128,2560]{3,2,1,0:T(8,128)(2,1)} %get-tuple-element.185, s32[]{:T(128)} %get-tuple-element.174), kind=kOutput, calls=%fused_computation.8.clone.1 | convolution fusion | flops 1746534400 | bytes 19022336 | tf_op jit(solution)/shard_map/while/body/eval_jaxpr/vmap(bfs,ks->fbk)/dot_general | solution.py:83
  228.7 1.0 fusion.82
  229.7 8.7 %slice.31 = bf16[16,4,5248]{2,1,0:T(4,128)(2,1)S(1)} slice(bf16[16,16,5248]{2,1,0:T(8,128)(2,1)} %bitcast.73), slice={[0:16:1], [0:16:4], [0:5248:1]} | slice | bytes 1343488 | tf_op jit(solution)/shard_map/slice | solution.py:121
  238.6 4.0 %fusion.69 = f32[16,4,5248]{2,0,1:T(8,128)S(1)} fusion(f32[16,4,5248]{2,0,1:T(8,128)S(1)} %rev.17), kind=kOutput, calls=%fused_computation.126 | output fusion | flops 1007616 | bytes 2686976 | tf_op jit(solution)/shard_map/jit(cumsum)/reduce_window_sum | solution.py:128
  242.7 0.7 slice.39
  243.5 22.9 %all-gather.3.cloned.1.call-done = f32[64,1,5248]{2,0,1:T(8,128)} async-done(((f32[16,1,5248]{2,0,1:T(8,128)}), f32[64,1,5248]{2,0,1:T(8,128)}) %all-gather.3.cloned.1.call-update) | async-done | bytes 1343504 | tf_op jit(solution)/shard_map/all_gather | solution.py:129
  266.4 1.5 multiply_reduce_fusion
  268.0 1.1 copy.38
  (57 shorter events, 4.3 us)
Async XLA Ops:
  7.2 3.3 %copy-start.1 = (bf16[2,2]{1,0:T(2,128)(2,1)S(1)}, bf16[2,2]{1,0:T(2,128)(2,1)}, u32[]{:S(2)}) copy-start(bf16[2,2]{1,0:T(2,128)(2,1)} %constant.93.clone) | copy-start | bytes 28
  57.5 12.5 %copy-start.3 = (s32[512]{0:T(512)S(1)}, s32[512]{0:T(512)}, u32[]{:S(2)}) copy-start(s32[512]{0:T(512)} %param.11) | copy-start | bytes 6148
  57.5 12.7 %copy-start.2 = (s32[640]{0:T(1024)S(1)}, s32[640]{0:T(1024)}, u32[]{:S(2)}) copy-start(s32[640]{0:T(1024)} %param.10) | copy-start | bytes 7684
  57.5 14.0 %copy-start.4 = (f32[16]{0:T(128)S(1)}, f32[16]{0:T(128)}, u32[]{:S(2)}) copy-start(f32[16]{0:T(128)} %param.12) | copy-start | bytes 196
  57.5 86.1 %all-to-all-start = ((f32[64,20,512]{2,1,0:T(8,128)}), f32[64,20,512]{2,1,0:T(8,128)S(1)}, u32[]{:S(2)}, u32[]{:S(2)}) async-start(f32[64,20,512]{2,1,0:T(8,128)} %copy.34), calls=%async_computation | async-start | bytes 6291456 | tf_op jit(solution)/shard_map/all_to_all | solution.py:111
  69.8 196.6 %all-gather.3.cloned.1.call-start = ((), (), s32[]{:S(2)}) async-start(), calls=%async_computation.1 | async-start | bytes 1679360 | tf_op jit(solution)/shard_map/all_gather | solution.py:129
  71.6 8.0 %copy-start = (s32[8,1280]{1,0:T(8,128)S(1)}, s32[8,1280]{1,0:T(8,128)}, u32[]{:S(2)}) copy-start(s32[8,1280]{1,0:T(8,128)} %get-tuple-element.100) | copy-start | bytes 122884
Sparse Core Ops, SparseCore 0:
  243.6 22.7 all-gather.2

commit v2 on v1

--- a/solution.py
+++ b/solution.py
@@ -2,6 +2,8 @@
 import jax.numpy as jnp
 from jax import lax
 from jax.sharding import PartitionSpec as P
+from jax.experimental import pallas as pl
+from jax.experimental.pallas import tpu as pltpu
 
 TRUNC = 1279
 QUANTITY_COUNT = 4
@@ -64,27 +66,79 @@
     )
     wave_limit = jnp.minimum(TRUNC, (lengths - 1) // 2)
     keep = (wave_numbers[None, :] <= wave_limit[:, None]).astype(jnp.float32)[:, None, :]
-    cos_t = cos_t.reshape(rows, 48, slots)[:, :BLOCKS] * keep
-    sin_t = sin_t.reshape(rows, 48, slots)[:, :BLOCKS] * keep
+    live = (jnp.arange(48) < BLOCKS).astype(jnp.float32)[None, :, None] * keep
+    cos_t = cos_t.reshape(rows, 48, slots) * live
+    sin_t = sin_t.reshape(rows, 48, slots) * live
     return base_t, cos_t, sin_t
 
 
-def synth_row(pack):
-    fourier_row, base_t, cos_t, sin_t, points = pack
-    fields = fourier_row.shape[0] // 2
-    real_part = fourier_row[:fields]
-    imag_part = fourier_row[fields:]
-    c = cos_t[:, None, :]
-    s = sin_t[:, None, :]
-    twisted = jnp.concatenate(
-        [real_part[None] * c - imag_part[None] * s, real_part[None] * s + imag_part[None] * c],
-        axis=2,
-    ).astype(jnp.bfloat16)
-    values = jnp.einsum("bfs,ks->fbk", twisted, base_t, preferred_element_type=jnp.float32)
-    values = values.reshape(fields, LCAP)
-    position = jnp.arange(LCAP, dtype=jnp.int32)
-    values = jnp.where(position[None, :] < points, values, 0.0)
-    return values.astype(jnp.bfloat16)
+def main_kernel(lengths_ref, rowmap_ref, f_ref, base_ref, cos_ref, sin_ref, out_ref, tw_ref):
+    r = pl.program_id(0)
+    points = lengths_ref[r]
+    fields = out_ref.shape[1]
+    slots = f_ref.shape[2]
+    real_part = f_ref[0, 0:fields, :]
+    imag_part = f_ref[0, fields:2 * fields, :]
+    for b in range(BLOCKS):
+        c = cos_ref[0, b:b + 1, :]
+        s = sin_ref[0, b:b + 1, :]
+        rows = slice(fields * b, fields * (b + 1))
+        tw_ref[rows, 0:slots] = (real_part * c - imag_part * s).astype(jnp.bfloat16)
+        tw_ref[rows, slots:2 * slots] = (real_part * s + imag_part * c).astype(jnp.bfloat16)
+    values = lax.dot_general(tw_ref[...], base_ref[0], (((1,), (1,)), ((), ())),
+                             preferred_element_type=jnp.float32)
+    lane = lax.broadcasted_iota(jnp.int32, (fields, BLOCK), 1)
+    for b in range(BLOCKS):
+        v = values[fields * b:fields * (b + 1), :]
+        v = jnp.where(lane + BLOCK * b < points, v, 0.0)
+        out_ref[0, :, BLOCK * b:BLOCK * (b + 1)] = v.astype(jnp.bfloat16)
+
+
+def heat_kernel(lengths_ref, rowmap_ref, f_ref, base_ref, cos_ref, sin_ref, out_ref, tw_ref):
+    r = pl.program_id(0)
+    points = lengths_ref[r]
+    fields = out_ref.shape[1]
+    slots = f_ref.shape[2]
+    depth = cos_ref.shape[1]
+    c = cos_ref[0]
+    s = sin_ref[0]
+    for f in range(fields):
+        re = f_ref[0, f:f + 1, :]
+        im = f_ref[0, fields + f:fields + f + 1, :]
+        rows = slice(depth * f, depth * (f + 1))
+        tw_ref[rows, 0:slots] = (re * c - im * s).astype(jnp.bfloat16)
+        tw_ref[rows, slots:2 * slots] = (re * s + im * c).astype(jnp.bfloat16)
+    values = lax.dot_general(tw_ref[...], base_ref[0], (((1,), (1,)), ((), ())),
+                             preferred_element_type=jnp.float32)
+    lane = lax.broadcasted_iota(jnp.int32, (1, BLOCK), 1)
+    for f in range(fields):
+        for b in range(BLOCKS):
+            v = values[depth * f + b:depth * f + b + 1, :]
+            v = jnp.where(lane + BLOCK * b < points, v, 0.0)
+            out_ref[0, f:f + 1, BLOCK * b:BLOCK * (b + 1)] = v.astype(jnp.bfloat16).astype(jnp.float32)
+
+
+def synth(kernel, fourier, base_t, cos_t, sin_t, lengths, rowmap, fields, out_dtype, tw_rows):
+    rows, cols, slots = fourier.shape
+    depth = cos_t.shape[1]
+    grid_spec = pltpu.PrefetchScalarGridSpec(
+        num_scalar_prefetch=2,
+        grid=(rows,),
+        in_specs=[
+            pl.BlockSpec((1, cols, slots), lambda r, n, m: (m[r], 0, 0)),
+            pl.BlockSpec((1, BLOCK, 2 * slots), lambda r, n, m: (r, 0, 0)),
+            pl.BlockSpec((1, depth, slots), lambda r, n, m: (r, 0, 0)),
+            pl.BlockSpec((1, depth, slots), lambda r, n, m: (r, 0, 0)),
+        ],
+        out_specs=pl.BlockSpec((1, fields, LCAP), lambda r, n, m: (r, 0, 0)),
+        scratch_shapes=[pltpu.VMEM((tw_rows, 2 * slots), jnp.bfloat16)],
+    )
+    return pl.pallas_call(
+        kernel,
+        grid_spec=grid_spec,
+        out_shape=jax.ShapeDtypeStruct((rows, fields, LCAP), out_dtype),
+        compiler_params=pltpu.CompilerParams(dimension_semantics=("arbitrary",)),
+    )(lengths, rowmap, fourier, base_t, cos_t, sin_t)
 
 
 def local(coefficients, legendre, pair_wave, row_points, layer_logpressure_factor):
@@ -103,22 +157,31 @@
     selected = coef[:, :, None, :, :] * selection[:, :, :, None, :]
     signs = jnp.array([[1.0, 1.0], [1.0, -1.0]], jnp.bfloat16)
     lhs = signs[None, :, :, None, None, None] * selected[:, None]
-    sums = jnp.einsum("qaehci,qeit->atqhc", lhs, legendre, preferred_element_type=jnp.float32)
-    sums = sums.reshape(2, half_bands, band_rows, pair_local * 2, cols)
-    south = jnp.flip(sums[1], (0, 1))
-    bands = jnp.concatenate([sums[0], south], 0)
-    send = bands.transpose(0, 2, 1, 3).reshape(wave_count, pair_local * 2, band_rows * cols)
+    sums = jnp.einsum("qaehci,qeit->qahct", lhs, legendre, preferred_element_type=jnp.float32)
+    sums = sums.reshape(pair_local, 2, 2, cols, half_bands, band_rows)
+    north = sums[:, 0]
+    south = jnp.flip(sums[:, 1], 3)
+    bands = jnp.concatenate([north, south], 3)
+    send = bands.transpose(3, 0, 1, 4, 2).reshape(wave_count, pair_local * 2, band_rows * cols)
     got = lax.all_to_all(send, "wave", 0, 0, tiled=True)
     slots = got.shape[0] * got.shape[1]
     fourier = got.reshape(slots, band_rows * cols).T.reshape(band_rows, cols, slots)
+    south_side = (wave_rank >= half_bands).astype(jnp.int32)
+    local_rows = jnp.arange(band_rows, dtype=jnp.int32)
+    rowmap = local_rows + south_side * (band_rows - 1 - 2 * local_rows)
 
     wave_numbers = jnp.stack([pair_wave, TRUNC - pair_wave], axis=1).reshape(-1)
     points_all = jnp.concatenate([row_points, jnp.flip(row_points)])
     lengths = lax.dynamic_slice_in_dim(points_all, wave_rank * band_rows, band_rows)
     base_t, cos_t, sin_t = tables(wave_numbers, lengths)
-    values = lax.map(synth_row, (fourier, base_t, cos_t, sin_t, lengths), batch_size=4)
-
-    heat_state_values = values[:, 0::QUANTITY_COUNT, :].astype(jnp.float32)
+    heat_cols = fourier.reshape(band_rows, 2, fields // QUANTITY_COUNT, QUANTITY_COUNT, slots)[:, :, :, 0]
+    heat_cols = heat_cols.reshape(band_rows, 2 * fields // QUANTITY_COUNT, slots)
+    heat_fields = fields // QUANTITY_COUNT
+    heat_state_values = synth(heat_kernel, heat_cols, base_t, cos_t, sin_t, lengths, rowmap,
+                              heat_fields, jnp.float32, heat_fields * 48)
+    values = synth(main_kernel, fourier, base_t, cos_t, sin_t, lengths, rowmap,
+                   fields, jnp.bfloat16, fields * BLOCKS)
+
     device_layers = heat_state_values.shape[1]
     lev_rank = lax.axis_index("lev")
     layer_depth_factor = lax.dynamic_slice_in_dim(

time: 278 us -> 212 us (0.76)
  Pallas kernels: 0 us -> 38.5 us
  other arithmetic: 81.3 us -> 46.4 us
  matrix products: 40.9 us -> 9.83 us
  waiting for transfers between devices: 64.9 us -> 43.4 us
  local copies, waits for them, and re-layouts: 61.9 us -> 46 us
    pallas_call x0 -> x2, Pallas kernels: none -> 38.5 us  [synth(): pl.pallas_call(kernel, grid_spec=grid_spec, out_shape=jax.ShapeDtypeStruc...]
    dot_general x5 -> x1, matrix products: 40.9 us -> 9.83 us  [local(): jnp.einsum('qaehci,qeit->qahct', lhs, legendre, preferred_element_type=jn...]
    another operation x5 -> x1, other arithmetic: 34.4 us -> 4.62 us
    all_gather x1, waiting for transfers between devices: 22.9 us -> 0.01 us  [local(): everything = lax.all_gather(partial_totals[:, 0, :], 'lev')]
    slice x8 -> x1, local copies, waits for them, and re-layouts: 16.4 us -> 3.6 us  [local(): fourier.reshape(band_rows, 2, fields // QUANTITY_COUNT, QUANTITY_COUNT, s...]
    mul x4 -> x0, local copies, waits for them, and re-layouts: 6.5 us -> none  [synth_row(): imag_part[None] * s]
    dynamic_update_slice x4 -> x0, other arithmetic: 4.05 us -> none  [local(): lax.map(synth_row, (fourier, base_t, cos_t, sin_t, lengths), batch_size=4)]
    another operation x0 -> x2, local copies, waits for them, and re-layouts: none -> 3.4 us  [the longest x1 2.34 us: local(): fourier.reshape(band_rows, 2, fields // QUANTITY_COUNT, QUANTITY_COUNT, s...]
  transfers between devices with their start and end apart: 2 -> 2, of which waited for: 2 -> 1; matrix products, arithmetic and copies ran while one was open for 11% -> 15% of each run, Pallas kernels for 0% -> 10%
where the time goes in v2:
time: 212 us; the launch traced here: 211 us
  other arithmetic  46.4 us (22%)
  local copies, waits for them, and re-layouts  46 us (22%)
  waiting for transfers between devices  43.4 us (20%)
  Pallas kernels  38.5 us (18%)
  between operations  14.3 us (7%)
  starting transfers between devices  12.5 us (6%)
  matrix products  9.83 us (5%)
    all_to_all x1, waiting for transfers between devices, local(): got = lax.all_to_all(send, 'wave', 0, 0, tiled=True)  43.4 us
    pallas_call x2, Pallas kernels, synth(): pl.pallas_call(kernel, grid_spec=grid_spec, out_shape=jax.ShapeDtypeStruc...  38.5 us
    cos x3, other arithmetic, phase(): return (jnp.cos(angle), jnp.sin(angle))  13.3 us
    all_to_all x1, starting transfers between devices, local(): got = lax.all_to_all(send, 'wave', 0, 0, tiled=True)  12.2 us
    dot_general x1, matrix products, local(): jnp.einsum('qaehci,qeit->qahct', lhs, legendre, preferred_element_type=jn...  9.83 us
    transpose x1, local copies, waits for them, and re-layouts, local(): bands.transpose(3, 0, 1, 4, 2)  9.46 us
    transpose x1, other arithmetic, local(): bands.transpose(3, 0, 1, 4, 2)  9.11 us
    concatenate x1, other arithmetic, tables(): jnp.concatenate([cos_b.reshape(rows, BLOCK, slots), -sin_b.reshape(rows,...  7.03 us
  transfers between devices with their start and end apart: 2, of which 1 were waited for; matrix products, arithmetic and copies ran while one was open for 15% of the time, Pallas kernels for 10%

profile of v2, /device:TPU:2, one launch (start us, length us, event | category | flops | bytes accessed | tf_op | source)
XLA Modules:
  0.0 210.9 jit_solution(4312949120216320563)
XLA Ops:
  7.2 0.0 copy-start.5
  7.2 1.9 copy.25
  9.1 0.1 copy.26
  9.2 0.8 broadcast_subtract_fusion.1
  10.0 0.1 fusion.38
  10.0 0.1 iota_compare_fusion
  10.2 0.1 add_convert_fusion.1
  10.3 0.2 broadcast_multiply_fusion
  10.5 0.0 copy-done.5
  10.5 9.8 %fusion = f32[10,2,2,32,512,1]{3,4,5,2,1,0:T(8,128)S(1)} fusion(bf16[10,2,640,512]{3,2,1,0:T(8,128)(2,1)} %param.7, bf16[10,2,2,32,640]{4,3,1,2,0:T(8,128)(2,1)S(1)} %broadcast_multiply_fusion, bf16[2,2]{1,0:T(2,128)(2,1)S(1)} %copy-done.5), kind=kOutput, calls=%fused_computation | convolution fusion | flops 1679360000 | bytes 17367048 | tf_op jit(solution)/shard_map/qaehci,qeit->qahct/dot_general | solution.py:160
  20.3 4.7 %slice_bitcast_fusion.1 = (f32[10,2,32,32,16]{2,4,3,1,0:T(8,128)}, f32[10,2,32,32,16]{2,4,3,1,0:T(8,128)}) fusion(f32[10,2,2,32,32,16]{3,5,4,2,1,0:T(8,128)S(1)} %bitcast.34), kind=kLoop, calls=%fused_computation.9 | loop fusion | bytes 5242880 | tf_op jit(solution)/shard_map/squeeze | solution.py:162
  25.0 5.3 %rev.16 = f32[10,2,32,32,16]{2,4,3,1,0:T(8,128)} reverse(f32[10,2,32,32,16]{2,4,3,1,0:T(8,128)} %get-tuple-element.7), dimensions={3} | reverse | bytes 2621440 | tf_op jit(solution)/shard_map/jit(_flip)/rev | solution.py:163
  30.3 9.1 %maximum_bitcast_fusion = f32[64,10,2,16,32]{4,3,0,2,1:T(8,128)} fusion(f32[10,2,32,32,16]{2,4,3,1,0:T(8,128)} %rev.16, f32[10,2,32,32,16]{2,4,3,1,0:T(8,128)} %get-tuple-element.6), kind=kLoop, calls=%fused_computation.2 | loop fusion | flops 655360 | bytes 5242880 | tf_op jit(solution)/shard_map/transpose | solution.py:165
  39.4 9.5 %copy.29 = f32[64,10,2,16,32]{0,4,3,2,1:T(8,128)} copy(f32[64,10,2,16,32]{4,3,0,2,1:T(8,128)} %maximum_bitcast_fusion) | data formatting | bytes 5242880 | tf_op jit(solution)/shard_map/transpose | solution.py:165
  48.8 5.9 %copy.30 = f32[64,20,512]{2,1,0:T(8,128)} copy(f32[64,20,512]{0,2,1:T(8,128)} %bitcast.33) | data formatting | bytes 5242880 | tf_op jit(solution)/shard_map/reshape | solution.py:165
  54.7 12.2 %all-to-all-start = ((f32[64,20,512]{2,1,0:T(8,128)}), f32[64,20,512]{2,1,0:T(8,128)S(1)}, u32[]{:S(2)}, u32[]{:S(2)}) async-start(f32[64,20,512]{2,1,0:T(8,128)} %copy.30), calls=%async_computation | async-start | bytes 6291456 | tf_op jit(solution)/shard_map/all_to_all | solution.py:166
  67.0 0.2 all-gather.3.cloned.1.call-start
  67.2 0.1 rev.15
  67.3 0.6 fusion.46
  68.0 0.2 copy.32
  68.2 0.2 mul.425
  68.4 0.1 compare_convert_fusion
  68.5 0.1 dynamic_slice.11
  68.6 0.1 broadcast_multiply_fusion.3
  68.7 0.1 broadcast_multiply_fusion.2
  68.7 2.6 %fusion.28 = (f32[16,6,1280]{2,1,0:T(8,128)S(1)}, f32[16,6,1280]{2,1,0:T(8,128)S(1)}) fusion(f32[16]{0:T(128)S(1)} %broadcast_divide_fusion, s32[16]{0:T(128)S(1)} %get-tuple-element.3.lengths_ref, f32[16]{0:T(128)S(1)} %convert_element_type.161, f32[6,1280]{1,0:T(8,128)S(1)} %get-tuple-element.21, s32[6,1280]{1,0:T(8,128)S(1)} %get-tuple-element.20), kind=kLoop, calls=%fused_computation.53 | loop fusion | flops 1597440 | bytes 1044672 | tf_op jit(solution)/shard_map/cos | solution.py:40
  71.4 5.2 %fusion.26 = (f32[16,16,1280]{2,1,0:T(8,128)S(1)}, f32[16,16,1280]{2,1,0:T(8,128)S(1)}) fusion(f32[16]{0:T(128)S(1)} %broadcast_divide_fusion, s32[16]{0:T(128)S(1)} %get-tuple-element.3.lengths_ref, f32[16]{0:T(128)S(1)} %convert_element_type.161, f32[16,1280]{1,0:T(8,128)S(1)} %get-tuple-element.29, s32[16,1280]{1,0:T(8,128)S(1)} %get-tuple-element.28), kind=kLoop, calls=%fused_computation.51 | loop fusion | flops 4259840 | bytes 2785472 | tf_op jit(solution)/shard_map/cos | solution.py:40
  76.6 5.4 %fusion.30 = (f32[16,8,1280]{2,1,0:T(8,128)S(1)}, f32[16,8,1280]{2,1,0:T(8,128)S(1)}, f32[16,8,1280]{2,1,0:T(8,128)S(1)}, f32[16,8,1280]{2,1,0:T(8,128)S(1)}) fusion(f32[16]{0:T(128)S(1)} %broadcast_divide_fusion, s32[16]{0:T(128)S(1)} %get-tuple-element.3.lengths_ref, f32[16]{0:T(128)S(1)} %convert_element_type.161, f32[8,1280]{1,0:T(8,128)S(1)} %get-tuple-element.23, ...), kind=kLoop, calls=%fused_computation.55 | loop fusion | flops 4259840 | bytes 2785472 | tf_op jit(solution)/shard_map/cos | solution.py:40
  82.0 4.6 %subtract_convert_fusion = (bf16[16,8,16,1280]{3,2,1,0:T(8,128)(2,1)S(1)}, bf16[16,8,16,1280]{3,2,1,0:T(8,128)(2,1)S(1)}) fusion(f32[16,16,1280]{2,1,0:T(8,128)S(1)} %get-tuple-element.13, f32[16,8,1280]{2,1,0:T(8,128)S(1)} %get-tuple-element.32, f32[16,16,1280]{2,1,0:T(8,128)S(1)} %get-tuple-element.12, f32[16,8,1280]{2,1,0:T(8,128)S(1)} %get-tuple-element.33), kind=kLoop, calls=%fused_computation.5 | loop fusion | flops 23592960 | bytes 14417920 | tf_op jit(solution)/shard_map/convert.3
  86.6 7.0 %pad_maximum_fusion.base_ref = bf16[16,128,2560]{2,1,0:T(8,128)(2,1)} fusion(bf16[16,128,1280]{2,1,0:T(8,128)(2,1)S(1)} %bitcast.32, bf16[16,128,1280]{2,1,0:T(8,128)(2,1)S(1)} %bitcast.31), kind=kLoop, calls=%fused_computation.3 | loop fusion | flops 20971520 | bytes 20971520 | tf_op jit(solution)/shard_map/concatenate | solution.py:58
  93.7 3.8 %multiply_multiply_fusion = (f32[16,48,1280]{2,1,0:T(8,128)}, f32[16,48,1280]{2,1,0:T(8,128)}) fusion(f32[16,1280]{1,0:T(8,128)S(1)} %compare_convert_fusion, f32[48]{0:T(128)S(1)} %compare_convert_fusion.2, f32[16,8,1280]{2,1,0:T(8,128)S(1)} %get-tuple-element.17, f32[16,6,1280]{2,1,0:T(8,128)S(1)} %get-tuple-element.15, ...), kind=kLoop, calls=%fused_computation.6 | loop fusion | flops 8847360 | bytes 10240192 | tf_op jit(solution)/shard_map/mul | solution.py:71
  97.5 43.4 %all-to-all-done = f32[64,20,512]{2,1,0:T(8,128)S(1)} async-done(((f32[64,20,512]{2,1,0:T(8,128)}), f32[64,20,512]{2,1,0:T(8,128)S(1)}, u32[]{:S(2)}, u32[]{:S(2)}) %all-to-all-start) | async-done | bytes 2621472 | tf_op jit(solution)/shard_map/all_to_all | solution.py:166
  140.8 1.6 reshape.555
  142.5 2.1 %copy.31 = f32[512,1280]{1,0:T(8,128)S(1)} copy(f32[512,1280]{0,1:T(8,128)} %bitcast.35) | data formatting | bytes 5242880 | tf_op jit(solution)/shard_map/transpose | solution.py:168
  144.6 2.3 %reshape_reshape.3 = f32[16,2,4,4,1280]{4,3,2,1,0:T(4,128)} reshape(f32[512,1280]{1,0:T(8,128)S(1)} %copy.31) | data formatting | bytes 5242880 | tf_op jit(solution)/shard_map/reshape;reshape | solution.py:177
  147.0 3.6 %slice_reduce_fusion = f32[16,2,4,1280]{3,2,1,0:T(4,128)S(1)} fusion(f32[16,2,4,4,1280]{4,3,2,1,0:T(4,128)} %reshape_reshape.3), kind=kLoop, calls=%fused_computation.49 | loop fusion | bytes 1310720 | tf_op jit(solution)/shard_map/slice | solution.py:177
  150.6 1.1 reshape_squeeze.3.f_ref
  151.6 16.6 %shard_map.78 = f32[16,4,5248]{2,1,0:T(4,128)} custom-call(s32[16]{0:T(128)} %copy-done.2, s32[16]{0:T(128)} %get-tuple-element.38.rowmap_ref, f32[16,8,1280]{2,1,0:T(8,128)} %reshape_squeeze.3.f_ref, bf16[16,128,2560]{2,1,0:T(8,128)(2,1)} %pad_maximum_fusion.base_ref, f32[16,48,1280]{2,1,0:T(8,128)} %get-tuple-element.11.cos_ref, ...), custom_call_target="tpu_custom_call" | custom-call | tf_op jit(solution)/shard_map/pallas_call | solution.py:136
  168.3 1.6 broadcast_multiply_fusion.1
  169.9 2.5 %rev.17 = f32[16,4,5248]{2,1,0:T(4,128)S(1)} reverse(f32[16,4,5248]{2,1,0:T(4,128)S(1)} %broadcast_multiply_fusion.1), dimensions={1} | reverse | bytes 2686976 | tf_op jit(solution)/shard_map/jit(_flip)/rev | solution.py:191
  172.4 3.5 %reduce_window_sum.11 = f32[16,4,5248]{2,1,0:T(4,128)S(1)} reduce-window(f32[16,4,5248]{2,1,0:T(4,128)S(1)} %rev.17, f32[]{:T(128)} %constant.80.clone.1), window={size=1x4x1 pad=0_0x3_0x0_0}, to_apply=%region_0.1 | reduce-window | flops 1007616 | bytes 2686980 | tf_op jit(solution)/shard_map/jit(cumsum)/reduce_window_sum | solution.py:191
  175.8 1.1 slice.20
  176.9 0.0 all-gather.3.cloned.1.call-update
  176.9 2.5 %rev.18 = f32[16,4,5248]{2,1,0:T(4,128)S(1)} reverse(f32[16,4,5248]{2,1,0:T(4,128)S(1)} %reduce_window_sum.11), dimensions={1} | reverse | bytes 2686976 | tf_op jit(solution)/shard_map/jit(_flip)/rev | solution.py:191
  179.4 21.8 %shard_map.77 = bf16[16,16,5248]{2,1,0:T(8,128)(2,1)} custom-call(s32[16]{0:T(128)} %copy-done.2, s32[16]{0:T(128)} %get-tuple-element.38.rowmap_ref, f32[16,32,1280]{2,1,0:T(8,128)} %bitcast.30, bf16[16,128,2560]{2,1,0:T(8,128)(2,1)} %pad_maximum_fusion.base_ref, f32[16,48,1280]{2,1,0:T(8,128)} %get-tuple-element.11.cos_ref, ...), custom_call_target="tpu_custom_call" | custom-call | tf_op jit(solution)/shard_map/pallas_call | solution.py:136
  201.2 1.4 copy.38
  202.7 0.2 multiply_reduce_fusion
  202.8 1.2 add_convert_fusion
  (23 shorter events, 0.1 us)
Async XLA Ops:
  7.2 3.3 %copy-start.5 = (bf16[2,2]{1,0:T(2,128)(2,1)S(1)}, bf16[2,2]{1,0:T(2,128)(2,1)}, u32[]{:S(2)}) copy-start(bf16[2,2]{1,0:T(2,128)(2,1)} %constant.81.clone) | copy-start | bytes 28
  54.7 12.5 %copy-start.3 = (s32[512]{0:T(512)S(1)}, s32[512]{0:T(512)}, u32[]{:S(2)}) copy-start(s32[512]{0:T(512)} %param.9) | copy-start | bytes 6148
  54.7 13.2 %copy-start.1 = (s32[640]{0:T(1024)S(1)}, s32[640]{0:T(1024)}, u32[]{:S(2)}) copy-start(s32[640]{0:T(1024)} %param.8) | copy-start | bytes 7684
  54.7 13.8 %copy-start.4 = (f32[16]{0:T(128)S(1)}, f32[16]{0:T(128)}, u32[]{:S(2)}) copy-start(f32[16]{0:T(128)} %param.10) | copy-start | bytes 196
  54.7 86.1 %all-to-all-start = ((f32[64,20,512]{2,1,0:T(8,128)}), f32[64,20,512]{2,1,0:T(8,128)S(1)}, u32[]{:S(2)}, u32[]{:S(2)}) async-start(f32[64,20,512]{2,1,0:T(8,128)} %copy.30), calls=%async_computation | async-start | bytes 6291456 | tf_op jit(solution)/shard_map/all_to_all | solution.py:166
  67.0 134.3 %all-gather.3.cloned.1.call-start = ((), (), s32[]{:S(2)}) async-start(), calls=%async_computation.1 | async-start | bytes 1679360 | tf_op jit(solution)/shard_map/all_gather | solution.py:192
  67.9 14.1 %copy-start.2 = (s32[16]{0:T(128)}, s32[16]{0:T(128)S(1)}, u32[]{:S(2)}) copy-start(s32[16]{0:T(128)S(1)} %get-tuple-element.3.lengths_ref) | copy-start | bytes 196
  144.6 7.0 %copy-start = (f32[512,1280]{1,0:T(8,128)}, f32[512,1280]{1,0:T(8,128)S(1)}, u32[]{:S(2)}) copy-start(f32[512,1280]{1,0:T(8,128)S(1)} %copy.31) | copy-start | bytes 7864324
Sparse Core Ops, SparseCore 0:
  177.0 22.7 all-gather.2
